TPU v7x, 32 devices: a whole 2x2x4 slice. The times are simulated.
32 devices in a mesh: row: 2 (over x), col: 4 (over z), tok: 4 (over y, core).
Axes of the slice: x: 2, y: 2, z: 4, core: 2. Of those that a mesh axis runs over, the one named last changes fastest.
Arguments:
- activations: bfloat16 [4096, 2048], P(('row', 'col', 'tok')), may hold values from -6 to 6
- norm_gain: float32 [2048], replicated, may hold values from 0.1 to 1.9
- routes: int32 [4096, 8], P(('row', 'col', 'tok')), may hold values from 0 to 127, all different within a row; in each aligned block of 128 rows (0 to 127, 128 to 255, ...) at most 10 rows name the same one
- route_weights: float32 [4096, 8], P(('row', 'col', 'tok')), may hold values from 0.05 to 1
- gate_up_weight: bfloat16 [128, 2, 768, 2048], P(('row', 'col'), None, 'tok'), may hold values from -0.125 to 0.125
- down_weight: bfloat16 [128, 768, 2048], P(('row', 'col'), 'tok'), may hold values from -0.21875 to 0.21875
Outputs:
- expert_mix: bfloat16 [4096, 2048], P(('row', 'col', 'tok'))
Inputs may be any that keep to these rules, and one draw needn't show every extreme that they name: `routes`: within the rows of one device no expert is named by more than 10 rows, a bound that some block reaches.
All inputs are finite; a program needn't handle non-finite values.
Results may differ from a plain program's by a relative error of at most 0.0085.
Values may be sent and summed in bfloat16 or wider, within the bound.
No kernel may reach another device: no remote copies, remote signals or barrier semaphores. Data moves between devices by JAX's collectives and lax.ppermute only.
A program may use at most 384 MiB of HBM per device.

v0:
```python
import math
import jax
import jax.numpy as jnp
from jax import lax
from jax.sharding import PartitionSpec as P

CAP = 10
PIECES = 4
EPSILON = 1e-06
ALL = ("row", "col", "tok")


def rank_in_block(block_routes, experts):
    onehot = (block_routes[:, None] == jnp.arange(experts, dtype=jnp.int32)[None, :]).astype(
        jnp.int32
    )
    before = jnp.cumsum(onehot, axis=0) - onehot
    return jnp.sum(before * onehot, axis=1)


def rms_normed(activations, norm_gain):
    values = activations.astype(jnp.float32)
    scale = lax.rsqrt(jnp.mean(values * values, axis=-1, keepdims=True) + EPSILON)
    return (values * scale * norm_gain).astype(jnp.bfloat16)


def local(activations, norm_gain, routes, route_weights, gate_up_weight, down_weight):
    count, features = activations.shape
    chosen = routes.shape[1]
    holding = gate_up_weight.shape[0]
    row_count = lax.axis_size("row")
    col_count = lax.axis_size("col")
    tok_count = lax.axis_size("tok")
    owners = row_count * col_count
    experts = holding * owners
    devices = owners * tok_count
    owner = lax.axis_index("row") * col_count + lax.axis_index("col")
    assert count < 256
    normed = rms_normed(activations, norm_gain)
    gates = route_weights / jnp.sum(route_weights, axis=1, keepdims=True)
    flat_routes = routes.reshape(-1)
    target = flat_routes * CAP + rank_in_block(flat_routes, experts)
    token_ids = jnp.arange(count * chosen, dtype=jnp.int32) // chosen
    source = jnp.full((experts * CAP,), count, jnp.int32).at[target].set(token_ids)
    extra = -(-(experts * CAP) // features)
    extra = -(-extra // 8) * 8
    stride = count + extra
    table_rows = jnp.zeros((extra * features,), jnp.bfloat16)
    table_rows = table_rows.at[: experts * CAP].set(source.astype(jnp.bfloat16))
    packed = jnp.concatenate([normed, table_rows.reshape(extra, features)], axis=0)
    every = lax.all_gather(packed, ALL, axis=0, tiled=True)
    tables = every.reshape(devices, stride, features)[:, count:, :].reshape(devices, -1)
    tables = lax.dynamic_slice_in_dim(
        tables[:, : experts * CAP], owner * holding * CAP, holding * CAP, axis=1
    ).astype(jnp.int32)
    rows = tables + (jnp.arange(devices, dtype=jnp.int32) * stride)[:, None]
    rows = rows.reshape(owners, tok_count, holding, CAP).transpose(2, 1, 0, 3).reshape(-1)
    rows = rows.reshape(holding, -1)
    pieces = math.gcd(holding, PIECES)
    width = holding // pieces
    returned = []
    sums = []
    for piece in range(pieces):
        span = slice(piece * width, (piece + 1) * width)
        picked = jnp.take(every, rows[span].reshape(-1), axis=0, mode="clip")
        picked = picked.reshape(width, tok_count * owners * CAP, features)
        both = jnp.einsum(
            "jrd,jgfd->jrgf", picked, gate_up_weight[span], preferred_element_type=jnp.float32
        )
        hidden = (jax.nn.silu(both[:, :, 0, :]) * both[:, :, 1, :]).astype(jnp.bfloat16)
        partial = jnp.einsum(
            "jrf,jfd->jrd", hidden, down_weight[span], preferred_element_type=jnp.float32
        )
        partial = partial.astype(jnp.bfloat16)
        if sums:
            partial, _ = lax.optimization_barrier((partial, (sums[-1], returned[:-1])))
        sums.append(lax.psum_scatter(partial, "tok", scatter_dimension=1, tiled=True))
        summed = sums[-1].reshape(width, owners, CAP, features).transpose(1, 0, 2, 3)
        summed = summed.reshape(owners, width * CAP, features)
        returned.append(
            lax.all_to_all(summed, ("row", "col"), split_axis=0, concat_axis=0, tiled=True)
        )
    returned = jnp.concatenate(returned, axis=1)
    picked_back = jnp.take(returned.reshape(experts * CAP, features), target, axis=0)
    picked_back = picked_back.reshape(count, chosen, features)
    mixed = jnp.einsum("tk,tkd->td", gates, picked_back.astype(jnp.float32))
    return mixed.astype(jnp.bfloat16)


def solution(mesh):
    in_specs = (
        P(("row", "col", "tok"), None),
        P(),
        P(("row", "col", "tok"), None),
        P(("row", "col", "tok"), None),
        P(("row", "col"), None, "tok", None),
        P(("row", "col"), "tok", None),
    )
    out_specs = P(("row", "col", "tok"), None)
    return jax.shard_map(local, mesh=mesh, in_specs=in_specs, out_specs=out_specs, check_vma=False)
```

profile of v0, /device:TPU:0, one launch (start us, length us, event | category | flops | bytes accessed | tf_op | source)
XLA Modules:
  0.0 457.8 jit_solution(16420601011597710427)
XLA Ops:
  6.5 0.7 broadcast_multiply_fusion
  7.3 0.8 copy.68
  8.3 1.2 fusion.23
  10.6 4.3 scatter_custom_fusion
  15.2 0.9 pad_maximum_fusion.1
  16.2 122.6 %all-gather.2.cloned.1.call-done = bf16[4352,2048]{1,0:T(8,128)(2,1)} async-done(((bf16[136,2048]{1,0:T(8,128)(2,1)}), bf16[4352,2048]{1,0:T(8,128)(2,1)}) %all-gather.2.cloned.1.call-update) | async-done | bytes 17825808 | tf_op jit(solution)/shard_map/all_gather | solution.py:51
  138.8 1.3 slice.123
  140.1 0.6 copy.108
  141.2 19.2 %gather_fusion = bf16[1280,2048]{1,0:T(8,128)(2,1)} fusion(bf16[4352,2048]{1,0:T(8,128)(2,1)} %all-gather.2.cloned.1.call-done, s32[2048]{0:T(1024)S(1)} %pad_clamp_fusion.3), kind=kCustom, calls=%fused_computation | custom fusion | bytes 10490880 | tf_op jit(solution)/shard_map/jit(_take)/gather | solution.py:65
  160.4 7.8 %fusion.6 = f32[4,320,2,192]{1,3,2,0:T(8,128)S(1)} fusion(bf16[4,320,2048,1]{2,1,3,0:T(8,128)(2,1)} %bitcast.124, bf16[16,2,192,2048]{3,2,1,0:T(8,128)(2,1)} %param.12), kind=kOutput, calls=%fused_computation.12 | convolution fusion | flops 2013265920 | bytes 13500416 | tf_op jit(solution)/shard_map/jrd,jgfd->jrgf/dot_general | solution.py:67
  168.2 5.8 %convolution_convert_fusion.3 = bf16[4,320,2048]{2,1,0:T(8,128)(2,1)} fusion(bf16[16,192,2048]{2,1,0:T(8,128)(2,1)} %param.13, f32[4,320,2,192]{1,3,2,0:T(8,128)S(1)} %fusion.6), kind=kOutput, calls=%fused_computation.21 | convolution fusion | flops 1010728960 | bytes 10354688 | tf_op jit(solution)/shard_map/jrf,jfd->jrd/dot_general | solution.py:71
  174.2 16.3 %fusion.49 = (bf16[4,2,192,2048]{3,2,1,0:T(8,128)(2,1)}, bf16[4,2,192,2048]{3,2,1,0:T(8,128)(2,1)}, bf16[4,2,192,2048]{3,2,1,0:T(8,128)(2,1)}) fusion(bf16[16,2,192,2048]{3,2,1,0:T(8,128)(2,1)} %param.12), kind=kLoop, calls=%fused_computation.91 | loop fusion | bytes 37748736 | tf_op jit(solution)/shard_map/slice | solution.py:68
  190.6 20.0 %gather_fusion.1 = bf16[1280,2048]{1,0:T(8,128)(2,1)} fusion(bf16[4352,2048]{1,0:T(8,128)(2,1)} %all-gather.2.cloned.1.call-done, s32[2048]{0:T(1024)S(1)} %pad_clamp_fusion.2), kind=kCustom, calls=%fused_computation.1 | custom fusion | bytes 10490880 | tf_op jit(solution)/shard_map/jit(_take)/gather | solution.py:65
  210.7 7.8 %fusion.4 = f32[4,320,2,192]{1,3,0,2:T(8,128)S(1)} fusion(bf16[4,320,2048,1]{2,1,0,3:T(8,128)(2,1)} %bitcast.122, bf16[4,2,192,2048]{3,2,1,0:T(8,128)(2,1)} %get-tuple-element.23), kind=kOutput, calls=%fused_computation.10 | convolution fusion | flops 2013265920 | bytes 13500416 | tf_op jit(solution)/shard_map/jrd,jgfd->jrgf/dot_general | solution.py:67
  218.5 5.8 %convolution_convert_fusion.2 = bf16[4,320,2048]{2,1,0:T(8,128)(2,1)} fusion(bf16[16,192,2048]{2,1,0:T(8,128)(2,1)} %param.13, f32[4,320,2,192]{1,3,0,2:T(8,128)S(1)} %fusion.4), kind=kOutput, calls=%fused_computation.20 | convolution fusion | flops 1010728960 | bytes 10354688 | tf_op jit(solution)/shard_map/jrf,jfd->jrd/dot_general | solution.py:71
  224.3 1.3 copy-done.2
  225.6 1.0 copy.77
  226.6 0.7 copy.78
  227.3 1.8 copy.79
  229.1 5.0 %all-to-all-start = ((bf16[8,40,2048]{2,1,0:T(8,128)(2,1)}), bf16[8,40,2048]{2,1,0:T(8,128)(2,1)S(1)}, u32[]{:S(2)}, u32[]{:S(2)}) async-start(bf16[8,40,2048]{2,1,0:T(8,128)(2,1)} %copy.79), calls=%async_computation.1 | async-start | bytes 2621440 | tf_op jit(solution)/shard_map/all_to_all | solution.py:81
  234.5 20.5 %gather_fusion.2 = bf16[1280,2048]{1,0:T(8,128)(2,1)} fusion(bf16[4352,2048]{1,0:T(8,128)(2,1)} %all-gather.2.cloned.1.call-done, s32[2048]{0:T(1024)S(1)} %pad_clamp_fusion.1), kind=kCustom, calls=%fused_computation.2 | custom fusion | bytes 10490880 | tf_op jit(solution)/shard_map/jit(_take)/gather | solution.py:65
  255.0 7.9 %fusion.2 = f32[4,320,2,192]{1,3,0,2:T(8,128)S(1)} fusion(bf16[4,320,2048,1]{2,1,0,3:T(8,128)(2,1)} %bitcast.123, bf16[4,2,192,2048]{3,2,1,0:T(8,128)(2,1)} %get-tuple-element.25), kind=kOutput, calls=%fused_computation.8 | convolution fusion | flops 2013265920 | bytes 13500416 | tf_op jit(solution)/shard_map/jrd,jgfd->jrgf/dot_general | solution.py:67
  262.9 5.9 %convolution_convert_fusion.1 = bf16[4,320,2048]{2,1,0:T(8,128)(2,1)} fusion(bf16[16,192,2048]{2,1,0:T(8,128)(2,1)} %param.13, f32[4,320,2,192]{1,3,0,2:T(8,128)S(1)} %fusion.2), kind=kOutput, calls=%fused_computation.19 | convolution fusion | flops 1010728960 | bytes 10354688 | tf_op jit(solution)/shard_map/jrf,jfd->jrd/dot_general | solution.py:71
  268.8 9.1 %reduce-scatter.7.cloned.1.call-done = bf16[4,80,2048]{2,1,0:T(8,128)(2,1)} async-done(((bf16[4,320,2048]{2,1,0:T(8,128)(2,1)}), bf16[4,80,2048]{2,1,0:T(8,128)(2,1)}) %reduce-scatter.7.cloned.1.call-update) | async-done | bytes 1310736 | tf_op jit(solution)/shard_map/reduce_scatter | solution.py:77
  277.9 1.3 copy-done.1
  279.2 1.0 copy.83
  280.2 0.7 copy.84
  280.9 1.8 copy.85
  282.7 5.5 %all-to-all-start.1 = ((bf16[8,40,2048]{2,1,0:T(8,128)(2,1)}), bf16[8,40,2048]{2,1,0:T(8,128)(2,1)S(1)}, u32[]{:S(2)}, u32[]{:S(2)}) async-start(bf16[8,40,2048]{2,1,0:T(8,128)(2,1)} %copy.85), calls=%async_computation.3 | async-start | bytes 2621440 | tf_op jit(solution)/shard_map/all_to_all | solution.py:81
  288.2 0.4 reduce-scatter.11.cloned.1.call-start
  288.8 20.2 %gather_fusion.3 = bf16[1280,2048]{1,0:T(8,128)(2,1)} fusion(bf16[4352,2048]{1,0:T(8,128)(2,1)} %all-gather.2.cloned.1.call-done, s32[2048]{0:T(1024)S(1)} %pad_clamp_fusion), kind=kCustom, calls=%fused_computation.3 | custom fusion | bytes 10490880 | tf_op jit(solution)/shard_map/jit(_take)/gather | solution.py:65
  309.0 7.9 %fusion = f32[4,320,2,192]{1,3,0,2:T(8,128)S(1)} fusion(bf16[4,320,2048,1]{2,1,0,3:T(8,128)(2,1)} %bitcast.121, bf16[4,2,192,2048]{3,2,1,0:T(8,128)(2,1)} %get-tuple-element.24), kind=kOutput, calls=%fused_computation.6 | convolution fusion | flops 2013265920 | bytes 13500416 | tf_op jit(solution)/shard_map/jrd,jgfd->jrgf/dot_general | solution.py:67
  316.9 5.9 %convolution_convert_fusion = bf16[4,320,2048]{2,1,0:T(8,128)(2,1)} fusion(bf16[16,192,2048]{2,1,0:T(8,128)(2,1)} %param.13, f32[4,320,2,192]{1,3,0,2:T(8,128)S(1)} %fusion), kind=kOutput, calls=%fused_computation.18 | convolution fusion | flops 1010728960 | bytes 10354688 | tf_op jit(solution)/shard_map/jrf,jfd->jrd/dot_general | solution.py:71
  322.8 8.8 %reduce-scatter.9.cloned.1.call-done = bf16[4,80,2048]{2,1,0:T(8,128)(2,1)} async-done(((bf16[4,320,2048]{2,1,0:T(8,128)(2,1)}), bf16[4,80,2048]{2,1,0:T(8,128)(2,1)}) %reduce-scatter.9.cloned.1.call-update) | async-done | bytes 1310736 | tf_op jit(solution)/shard_map/reduce_scatter | solution.py:77
  331.7 2.3 copy.89
  334.0 0.7 copy.90
  334.7 1.9 copy.91
  336.6 5.8 %all-to-all-start.2 = ((bf16[8,40,2048]{2,1,0:T(8,128)(2,1)}), bf16[8,40,2048]{2,1,0:T(8,128)(2,1)}, u32[]{:S(2)}, u32[]{:S(2)}) async-start(bf16[8,40,2048]{2,1,0:T(8,128)(2,1)} %copy.91), calls=%async_computation.5 | async-start | bytes 2621440 | tf_op jit(solution)/shard_map/all_to_all | solution.py:81
  342.4 43.3 %reduce-scatter.11.cloned.1.call-done = bf16[4,80,2048]{2,1,0:T(8,128)(2,1)} async-done(((bf16[4,320,2048]{2,1,0:T(8,128)(2,1)}), bf16[4,80,2048]{2,1,0:T(8,128)(2,1)}) %reduce-scatter.11.cloned.1.call-update) | async-done | bytes 1310736 | tf_op jit(solution)/shard_map/reduce_scatter | solution.py:77
  385.6 2.3 copy.95
  388.0 0.7 copy.96
  388.7 1.8 copy.97
  390.5 5.5 %all-to-all-start.3 = ((bf16[8,40,2048]{2,1,0:T(8,128)(2,1)}), bf16[8,40,2048]{2,1,0:T(8,128)(2,1)}, u32[]{:S(2)}, u32[]{:S(2)}) async-start(bf16[8,40,2048]{2,1,0:T(8,128)(2,1)} %copy.97), calls=%async_computation.7 | async-start | bytes 2621440 | tf_op jit(solution)/shard_map/all_to_all | solution.py:81
  396.5 31.9 %all-to-all-done.3 = bf16[8,40,2048]{2,1,0:T(8,128)(2,1)} async-done(((bf16[8,40,2048]{2,1,0:T(8,128)(2,1)}), bf16[8,40,2048]{2,1,0:T(8,128)(2,1)}, u32[]{:S(2)}, u32[]{:S(2)}) %all-to-all-start.3) | async-done | bytes 1310752 | tf_op jit(solution)/shard_map/all_to_all | solution.py:81
  428.4 6.0 %pad_maximum_fusion = bf16[8,160,2048]{2,1,0:T(8,128)(2,1)} fusion(bf16[8,40,2048]{2,1,0:T(8,128)(2,1)} %all-to-all-done.3, bf16[8,40,2048]{2,1,0:T(8,128)(2,1)} %all-to-all-done.2, bf16[8,40,2048]{2,1,0:T(8,128)(2,1)S(1)} %all-to-all-done.1, bf16[8,40,2048]{2,1,0:T(8,128)(2,1)S(1)} %all-to-all-done), kind=kLoop, calls=%fused_computation.14 | loop fusion | flops 20971520 | bytes 10485760 | tf_op jit(solution)/shard_map/concatenate | solution.py:83
  434.4 12.0 %gather_fusion.4 = bf16[1024,2048]{1,0:T(8,128)(2,1)} fusion(bf16[1280,2048]{1,0:T(8,128)(2,1)} %bitcast.120, s32[1024]{0:T(1024)S(1)} %broadcast_clamp_fusion), kind=kCustom, calls=%fused_computation.4 | custom fusion | bytes 8392704 | tf_op jit(solution)/shard_map/jit(_take)/gather | solution.py:84
  446.4 3.5 fusion.8
  449.9 1.1 copy.116
  (67 shorter events, 3.5 us)
Async XLA Ops:
  6.5 8.4 %copy-start = (bf16[128,2048]{1,0:T(8,128)(2,1)S(1)}, bf16[128,2048]{1,0:T(8,128)(2,1)}, u32[]{:S(2)}) copy-start(bf16[128,2048]{1,0:T(8,128)(2,1)} %param.8) | copy-start | bytes 1572868
  6.5 8.5 %copy-start.5 = (f32[2048]{0:T(1024)S(1)}, f32[2048]{0:T(1024)}, u32[]{:S(2)}) copy-start(f32[2048]{0:T(1024)} %param.9) | copy-start | bytes 24580
  6.5 132.2 %all-gather.2.cloned.1.call-start = ((), (), s32[]{:S(2)}) async-start(), calls=%async_computation.8 | async-start | bytes 18382848 | tf_op jit(solution)/shard_map/all_gather | solution.py:51
  16.1 208.2 %reduce-scatter.5.cloned.1.call-start = ((), (), s32[]{:S(2)}) async-start(), calls=%async_computation.9 | async-start | bytes 6553600 | tf_op jit(solution)/shard_map/reduce_scatter | solution.py:77
  174.0 103.9 %reduce-scatter.7.cloned.1.call-start = ((), (), s32[]{:S(2)}) async-start(), calls=%async_computation.10 | async-start | bytes 6553600 | tf_op jit(solution)/shard_map/reduce_scatter | solution.py:77
  224.2 1.3 copy-start.2
  229.1 39.7 %all-to-all-start = ((bf16[8,40,2048]{2,1,0:T(8,128)(2,1)}), bf16[8,40,2048]{2,1,0:T(8,128)(2,1)S(1)}, u32[]{:S(2)}, u32[]{:S(2)}) async-start(bf16[8,40,2048]{2,1,0:T(8,128)(2,1)} %copy.79), calls=%async_computation.1 | async-start | bytes 2621440 | tf_op jit(solution)/shard_map/all_to_all | solution.py:81
  234.1 97.6 %reduce-scatter.9.cloned.1.call-start = ((), (), s32[]{:S(2)}) async-start(), calls=%async_computation.11 | async-start | bytes 6553600 | tf_op jit(solution)/shard_map/reduce_scatter | solution.py:77
  277.8 1.3 copy-start.1
  282.7 40.1 %all-to-all-start.1 = ((bf16[8,40,2048]{2,1,0:T(8,128)(2,1)}), bf16[8,40,2048]{2,1,0:T(8,128)(2,1)S(1)}, u32[]{:S(2)}, u32[]{:S(2)}) async-start(bf16[8,40,2048]{2,1,0:T(8,128)(2,1)} %copy.85), calls=%async_computation.3 | async-start | bytes 2621440 | tf_op jit(solution)/shard_map/all_to_all | solution.py:81
  288.2 97.4 %reduce-scatter.11.cloned.1.call-start = ((), (), s32[]{:S(2)}) async-start(), calls=%async_computation.12 | async-start | bytes 6553600 | tf_op jit(solution)/shard_map/reduce_scatter | solution.py:77
  336.6 53.9 %all-to-all-start.2 = ((bf16[8,40,2048]{2,1,0:T(8,128)(2,1)}), bf16[8,40,2048]{2,1,0:T(8,128)(2,1)}, u32[]{:S(2)}, u32[]{:S(2)}) async-start(bf16[8,40,2048]{2,1,0:T(8,128)(2,1)} %copy.91), calls=%async_computation.5 | async-start | bytes 2621440 | tf_op jit(solution)/shard_map/all_to_all | solution.py:81
  388.0 8.2 %copy-start.4 = (f32[128,8]{0,1:T(8,128)S(1)}, f32[128,8]{0,1:T(8,128)}, u32[]{:S(2)}) copy-start(f32[128,8]{0,1:T(8,128)} %param.11) | copy-start | bytes 12292
  388.0 8.4 %copy-start.3 = (s32[128,8]{0,1:T(8,128)S(1)}, s32[128,8]{0,1:T(8,128)}, u32[]{:S(2)}) copy-start(s32[128,8]{0,1:T(8,128)} %param.10) | copy-start | bytes 12292
  390.5 37.9 %all-to-all-start.3 = ((bf16[8,40,2048]{2,1,0:T(8,128)(2,1)}), bf16[8,40,2048]{2,1,0:T(8,128)(2,1)}, u32[]{:S(2)}, u32[]{:S(2)}) async-start(bf16[8,40,2048]{2,1,0:T(8,128)(2,1)} %copy.97), calls=%async_computation.7 | async-start | bytes 2621440 | tf_op jit(solution)/shard_map/all_to_all | solution.py:81
Sparse Core Ops, SparseCore 0:
  16.2 122.5 all-gather.1
  174.1 49.5 reduce-scatter.4
  226.4 51.4 reduce-scatter.6
  280.2 51.3 reduce-scatter.8
  334.2 51.3 reduce-scatter.10
where the time goes:
time: 467 us; the launch traced here: 458 us
  waiting for transfers between devices  216 us (46%)
  local copies, waits for them, and re-layouts  138 us (30%)
  matrix products  58.2 us (12%)
  starting transfers between devices  22.7 us (5%)
  between operations  13.7 us (3%)
  other arithmetic  9.89 us (2%)
    all_gather x1, waiting for transfers between devices, local(): every = lax.all_gather(packed, ALL, axis=0, tiled=True)  123 us
    gather x4, local copies, waits for them, and re-layouts, local(): picked = jnp.take(every, rows[span].reshape(-1), axis=0, mode='clip')  79.9 us
    reduce_scatter x4, waiting for transfers between devices, local(): lax.psum_scatter(partial, 'tok', scatter_dimension=1, tiled=True)  61.2 us
    all_to_all x4, waiting for transfers between devices, local(): lax.all_to_all(summed, ('row', 'col'), split_axis=0, concat_axis=0, tiled...  31.9 us
    dot_general x4, matrix products, local(): jnp.einsum('jrd,jgfd->jrgf', picked, gate_up_weight[span], preferred_elem...  31.4 us
    dot_general x4, matrix products, local(): jnp.einsum('jrf,jfd->jrd', hidden, down_weight[span], preferred_element_t...  23.3 us
    all_to_all x4, starting transfers between devices, local(): lax.all_to_all(summed, ('row', 'col'), split_axis=0, concat_axis=0, tiled...  21.7 us
    slice x1, local copies, waits for them, and re-layouts, local(): gate_up_weight[span]  16.3 us
  transfers between devices with their start and end apart: 9, of which 5 were waited for; matrix products, arithmetic and copies ran while one was open for 30% of the time, Pallas kernels for 0%

commit v1 on v0

--- a/solution.py
+++ b/solution.py
@@ -1,3 +1,4 @@
+import functools
 import math
 import jax
 import jax.numpy as jnp
@@ -8,6 +9,40 @@
 PIECES = 4
 EPSILON = 1e-06
 ALL = ("row", "col", "tok")
+
+
+def _mix_rates(base_x, where_dim, here_x):
+    z2, base_arr = (base_x.shape[:where_dim], base_x.shape[where_dim + 1 :])
+    return jnp.moveaxis(base_x.reshape(*z2, here_x, -1, *base_arr), where_dim, 0)
+
+
+def search_shards(original, dim_at):
+    original = jnp.moveaxis(original, 0, dim_at)
+    block_out = original.shape
+    return original.reshape(
+        *block_out[:dim_at], block_out[dim_at] * block_out[dim_at + 1], *block_out[dim_at + 2 :]
+    )
+
+
+def strings_draft(buf, packet, w_in, comm_axis):
+    raw_out = lax.axis_size(comm_axis)
+    mixed_arr = lax.axis_index(comm_axis)
+    met_up, field_out = (raw_out, mixed_arr)
+    carry_in = _mix_rates(buf, w_in, met_up)
+    all_blocks = [carry_in[field_out]]
+    it = 1
+    while it < met_up:
+        reply = carry_in[field_out ^ it]
+        all_blocks.append(
+            lax.ppermute(reply, axis_name=comm_axis, perm=[(at, at ^ it) for at in range(met_up)])
+        )
+        it += 1
+    r_now = jnp.stack(all_blocks)
+    carry_in = r_now[field_out ^ jnp.arange(met_up)]
+    return search_shards(carry_in, packet)
+
+
+_pack_spans = functools.partial(strings_draft, packet=0, w_in=0, comm_axis=("row", "col"))
 
 
 def rank_in_block(block_routes, experts):
@@ -77,9 +112,7 @@
         sums.append(lax.psum_scatter(partial, "tok", scatter_dimension=1, tiled=True))
         summed = sums[-1].reshape(width, owners, CAP, features).transpose(1, 0, 2, 3)
         summed = summed.reshape(owners, width * CAP, features)
-        returned.append(
-            lax.all_to_all(summed, ("row", "col"), split_axis=0, concat_axis=0, tiled=True)
-        )
+        returned.append(_pack_spans(summed))
     returned = jnp.concatenate(returned, axis=1)
     picked_back = jnp.take(returned.reshape(experts * CAP, features), target, axis=0)
     picked_back = picked_back.reshape(count, chosen, features)

time: 467 us -> 501 us (1.073)
  local copies, waits for them, and re-layouts: 138 us -> 163 us
  starting transfers between devices: 22.7 us -> 47.5 us
  waiting for transfers between devices: 216 us -> 198 us
    ppermute x0 -> x28, waiting for transfers between devices: none -> 67.7 us  [strings_draft(): lax.ppermute(reply, axis_name=comm_axis, perm=[(at, at ^ it) for at in ra...]
    reduce_scatter x4, waiting for transfers between devices: 61.2 us -> 8.01 us  [local(): lax.psum_scatter(partial, 'tok', scatter_dimension=1, tiled=True)]
    ppermute x0 -> x28, starting transfers between devices: none -> 47.1 us  [strings_draft(): lax.ppermute(reply, axis_name=comm_axis, perm=[(at, at ^ it) for at in ra...]
    all_to_all x4 -> x0, waiting for transfers between devices: 31.9 us -> none  [local(): lax.all_to_all(summed, ('row', 'col'), split_axis=0, concat_axis=0, tiled...]
    all_to_all x4 -> x0, starting transfers between devices: 21.7 us -> none  [local(): lax.all_to_all(summed, ('row', 'col'), split_axis=0, concat_axis=0, tiled...]
    dynamic_slice x0 -> x4, local copies, waits for them, and re-layouts: none -> 12 us  [strings_draft(): reply = carry_in[field_out ^ it]]
    unnamed x14 -> x72, local copies, waits for them, and re-layouts: 3.98 us -> 15.9 us
    gather x0 -> x4, local copies, waits for them, and re-layouts: none -> 8.62 us  [strings_draft(): carry_in = r_now[field_out ^ jnp.arange(met_up)]]
  transfers between devices with their start and end apart: 9 -> 33, of which waited for: 5 -> 13; matrix products, arithmetic and copies ran while one was open for 30% -> 31% of each run, Pallas kernels for 0% -> 0%
where the time goes in v1:
time: 501 us; the launch traced here: 493 us
  waiting for transfers between devices  198 us (40%)
  local copies, waits for them, and re-layouts  163 us (33%)
  matrix products  59.1 us (12%)
  starting transfers between devices  47.5 us (9%)
  between operations  14.4 us (3%)
  other arithmetic  9.89 us (2%)
    all_gather x1, waiting for transfers between devices, local(): every = lax.all_gather(packed, ALL, axis=0, tiled=True)  123 us
    gather x4, local copies, waits for them, and re-layouts, local(): picked = jnp.take(every, rows[span].reshape(-1), axis=0, mode='clip')  78.9 us
    ppermute x28, waiting for transfers between devices, strings_draft(): lax.ppermute(reply, axis_name=comm_axis, perm=[(at, at ^ it) for at in ra...  67.7 us
    ppermute x28, starting transfers between devices, strings_draft(): lax.ppermute(reply, axis_name=comm_axis, perm=[(at, at ^ it) for at in ra...  47.1 us
    dot_general x4, matrix products, local(): jnp.einsum('jrd,jgfd->jrgf', picked, gate_up_weight[span], preferred_elem...  32.2 us
    dot_general x4, matrix products, local(): jnp.einsum('jrf,jfd->jrd', hidden, down_weight[span], preferred_element_t...  23.4 us
    slice x1, local copies, waits for them, and re-layouts, local(): gate_up_weight[span]  16.3 us
    unnamed x72, local copies, waits for them, and re-layouts  15.9 us
  transfers between devices with their start and end apart: 33, of which 13 were waited for; matrix products, arithmetic and copies ran while one was open for 31% of the time, Pallas kernels for 0%

profile of v1, /device:TPU:0, one launch (start us, length us, event | category | flops | bytes accessed | tf_op | source)
XLA Modules:
  0.0 492.5 jit_solution(13999375871100387799)
XLA Ops:
  10.6 4.3 scatter_custom_fusion
  16.1 122.6 %all-gather.2.cloned.1.call-done = bf16[4352,2048]{1,0:T(8,128)(2,1)} async-done(((bf16[136,2048]{1,0:T(8,128)(2,1)}), bf16[4352,2048]{1,0:T(8,128)(2,1)}) %all-gather.2.cloned.1.call-update) | async-done | bytes 17825808 | tf_op jit(solution)/shard_map/all_gather | solution.py:86
  141.3 19.2 %gather_fusion = bf16[1280,2048]{1,0:T(8,128)(2,1)} fusion(bf16[4352,2048]{1,0:T(8,128)(2,1)} %all-gather.2.cloned.1.call-done, s32[2048]{0:T(1024)S(1)} %get-tuple-element.65), kind=kCustom, calls=%fused_computation | custom fusion | bytes 10490880 | tf_op jit(solution)/shard_map/jit(_take)/gather | solution.py:100
  160.5 7.8 %fusion.6 = f32[4,320,2,192]{1,3,2,0:T(8,128)S(1)} fusion(bf16[4,320,2048,1]{2,1,3,0:T(8,128)(2,1)} %bitcast.330, bf16[16,2,192,2048]{3,2,1,0:T(8,128)(2,1)} %param.12), kind=kOutput, calls=%fused_computation.16 | convolution fusion | flops 2013265920 | bytes 13500416 | tf_op jit(solution)/shard_map/jrd,jgfd->jrgf/dot_general | solution.py:102
  168.3 5.8 %convolution_convert_fusion.3 = bf16[4,320,2048]{2,1,0:T(8,128)(2,1)} fusion(bf16[16,192,2048]{2,1,0:T(8,128)(2,1)} %param.13, f32[4,320,2,192]{1,3,2,0:T(8,128)S(1)} %fusion.6), kind=kOutput, calls=%fused_computation.25 | convolution fusion | flops 1010728960 | bytes 10354688 | tf_op jit(solution)/shard_map/jrf,jfd->jrd/dot_general | solution.py:106
  174.4 16.3 %fusion.50 = (bf16[4,2,192,2048]{3,2,1,0:T(8,128)(2,1)}, bf16[4,2,192,2048]{3,2,1,0:T(8,128)(2,1)}, bf16[4,2,192,2048]{3,2,1,0:T(8,128)(2,1)}) fusion(bf16[16,2,192,2048]{3,2,1,0:T(8,128)(2,1)} %param.12), kind=kLoop, calls=%fused_computation.190 | loop fusion | bytes 37748736 | tf_op jit(solution)/shard_map/slice | solution.py:103
  190.7 20.1 %gather_fusion.2 = bf16[1280,2048]{1,0:T(8,128)(2,1)} fusion(bf16[4352,2048]{1,0:T(8,128)(2,1)} %all-gather.2.cloned.1.call-done, s32[2048]{0:T(1024)S(1)} %get-tuple-element.64), kind=kCustom, calls=%fused_computation.2 | custom fusion | bytes 10490880 | tf_op jit(solution)/shard_map/jit(_take)/gather | solution.py:100
  210.7 7.8 %fusion.4 = f32[4,320,2,192]{1,3,0,2:T(8,128)S(1)} fusion(bf16[4,320,2048,1]{2,1,0,3:T(8,128)(2,1)} %bitcast.328, bf16[4,2,192,2048]{3,2,1,0:T(8,128)(2,1)} %get-tuple-element.23), kind=kOutput, calls=%fused_computation.14 | convolution fusion | flops 2013265920 | bytes 13500416 | tf_op jit(solution)/shard_map/jrd,jgfd->jrgf/dot_general | solution.py:102
  218.5 5.7 %convolution_convert_fusion.2 = bf16[4,320,2048]{2,1,0:T(8,128)(2,1)} fusion(bf16[16,192,2048]{2,1,0:T(8,128)(2,1)} %param.13, f32[4,320,2,192]{1,3,0,2:T(8,128)S(1)} %fusion.4), kind=kOutput, calls=%fused_computation.24 | convolution fusion | flops 1010728960 | bytes 10354688 | tf_op jit(solution)/shard_map/jrf,jfd->jrd/dot_general | solution.py:106
  224.7 19.6 %gather_fusion.4 = bf16[1280,2048]{1,0:T(8,128)(2,1)} fusion(bf16[4352,2048]{1,0:T(8,128)(2,1)} %all-gather.2.cloned.1.call-done, s32[2048]{0:T(1024)S(1)} %get-tuple-element.63), kind=kCustom, calls=%fused_computation.4 | custom fusion | bytes 10490880 | tf_op jit(solution)/shard_map/jit(_take)/gather | solution.py:100
  244.3 8.7 %fusion.2 = f32[4,320,2,192]{1,3,0,2:T(8,128)S(1)} fusion(bf16[4,320,2048,1]{2,1,0,3:T(8,128)(2,1)} %bitcast.329, bf16[4,2,192,2048]{3,2,1,0:T(8,128)(2,1)} %get-tuple-element.25), kind=kOutput, calls=%fused_computation.12 | convolution fusion | flops 2013265920 | bytes 13500416 | tf_op jit(solution)/shard_map/jrd,jgfd->jrgf/dot_general | solution.py:102
  253.0 5.9 %convolution_convert_fusion.1 = bf16[4,320,2048]{2,1,0:T(8,128)(2,1)} fusion(bf16[16,192,2048]{2,1,0:T(8,128)(2,1)} %param.13, f32[4,320,2,192]{1,3,0,2:T(8,128)S(1)} %fusion.2), kind=kOutput, calls=%fused_computation.23 | convolution fusion | flops 1010728960 | bytes 10354688 | tf_op jit(solution)/shard_map/jrf,jfd->jrd/dot_general | solution.py:106
  260.6 3.0 constant_dynamic-slice_fusion.23
  265.1 2.4 collective-permute-start.1
  270.4 4.1 collective-permute-done
  275.3 4.9 collective-permute-done.1
  280.2 3.3 collective-permute-start.6
  283.6 11.5 %collective-permute-done.5 = bf16[1,40,2048]{2,1,0:T(8,128)(2,1)S(1)} collective-permute-done((bf16[1,40,2048]{2,1,0:T(8,128)(2,1)S(1)}, bf16[1,40,2048]{2,1,0:T(8,128)(2,1)S(1)}, u32[]{:S(2)}, u32[]{:S(2)}) %collective-permute-start.5) | collective-permute-done | bytes 163872 | tf_op jit(solution)/shard_map/ppermute | solution.py:37
  295.8 20.1 %gather_fusion.6 = bf16[1280,2048]{1,0:T(8,128)(2,1)} fusion(bf16[4352,2048]{1,0:T(8,128)(2,1)} %all-gather.2.cloned.1.call-done, s32[2048]{0:T(1024)S(1)} %get-tuple-element.62), kind=kCustom, calls=%fused_computation.6 | custom fusion | bytes 10490880 | tf_op jit(solution)/shard_map/jit(_take)/gather | solution.py:100
  315.9 8.0 %fusion = f32[4,320,2,192]{1,3,0,2:T(8,128)S(1)} fusion(bf16[4,320,2048,1]{2,1,0,3:T(8,128)(2,1)} %bitcast.327, bf16[4,2,192,2048]{3,2,1,0:T(8,128)(2,1)} %get-tuple-element.24), kind=kOutput, calls=%fused_computation.10 | convolution fusion | flops 2013265920 | bytes 13500416 | tf_op jit(solution)/shard_map/jrd,jgfd->jrgf/dot_general | solution.py:102
  323.9 6.0 %convolution_convert_fusion = bf16[4,320,2048]{2,1,0:T(8,128)(2,1)} fusion(bf16[16,192,2048]{2,1,0:T(8,128)(2,1)} %param.13, f32[4,320,2,192]{1,3,0,2:T(8,128)S(1)} %fusion), kind=kOutput, calls=%fused_computation.22 | convolution fusion | flops 1010728960 | bytes 10354688 | tf_op jit(solution)/shard_map/jrf,jfd->jrd/dot_general | solution.py:106
  331.6 3.0 constant_dynamic-slice_fusion.15
  335.2 2.7 collective-permute-start.7
  340.7 2.1 collective-permute-start.11
  345.6 7.3 %collective-permute-done.8 = bf16[1,40,2048]{2,1,0:T(8,128)(2,1)S(1)} collective-permute-done((bf16[1,40,2048]{2,1,0:T(8,128)(2,1)S(1)}, bf16[1,40,2048]{2,1,0:T(8,128)(2,1)S(1)}, u32[]{:S(2)}, u32[]{:S(2)}) %collective-permute-start.8) | collective-permute-done | bytes 163872 | tf_op jit(solution)/shard_map/ppermute | solution.py:37
  353.0 2.2 collective-permute-start.13
  355.3 10.5 %collective-permute-done.12 = bf16[1,40,2048]{2,1,0:T(8,128)(2,1)S(1)} collective-permute-done((bf16[1,40,2048]{2,1,0:T(8,128)(2,1)S(1)}, bf16[1,40,2048]{2,1,0:T(8,128)(2,1)S(1)}, u32[]{:S(2)}, u32[]{:S(2)}) %collective-permute-start.12) | collective-permute-done | bytes 163872 | tf_op jit(solution)/shard_map/ppermute | solution.py:37
  369.9 2.3 copy.131
  373.0 3.2 constant_dynamic-slice_fusion.7
  376.7 2.4 collective-permute-start.14
  385.0 3.0 collective-permute-start.19
  388.8 5.4 %collective-permute-done.15 = bf16[1,40,2048]{2,1,0:T(8,128)(2,1)S(1)} collective-permute-done((bf16[1,40,2048]{2,1,0:T(8,128)(2,1)S(1)}, bf16[1,40,2048]{2,1,0:T(8,128)(2,1)S(1)}, u32[]{:S(2)}, u32[]{:S(2)}) %collective-permute-start.15) | collective-permute-done | bytes 163872 | tf_op jit(solution)/shard_map/ppermute | solution.py:37
  394.1 3.4 collective-permute-start.20
  400.2 7.8 %collective-permute-done.19 = bf16[1,40,2048]{2,1,0:T(8,128)(2,1)S(1)} collective-permute-done((bf16[1,40,2048]{2,1,0:T(8,128)(2,1)S(1)}, bf16[1,40,2048]{2,1,0:T(8,128)(2,1)S(1)}, u32[]{:S(2)}, u32[]{:S(2)}) %collective-permute-start.19) | collective-permute-done | bytes 163872 | tf_op jit(solution)/shard_map/ppermute | solution.py:37
  409.4 3.0 gather_fusion.5
  412.4 8.0 %reduce-scatter.11.cloned.1.call-done = bf16[4,80,2048]{2,1,0:T(8,128)(2,1)} async-done(((bf16[4,320,2048]{2,1,0:T(8,128)(2,1)}), bf16[4,80,2048]{2,1,0:T(8,128)(2,1)}) %reduce-scatter.11.cloned.1.call-update) | async-done | bytes 1310736 | tf_op jit(solution)/shard_map/reduce_scatter | solution.py:112
  420.4 2.3 copy.144
  423.5 3.0 constant_dynamic-slice_fusion.31
  428.5 2.4 collective-permute-start.22
  434.5 2.2 collective-permute-done.21
  436.6 2.3 collective-permute-start.26
  439.6 4.0 collective-permute-done.22
  443.6 3.4 collective-permute-start.27
  449.7 8.9 %collective-permute-done.26 = bf16[1,40,2048]{2,1,0:T(8,128)(2,1)S(1)} collective-permute-done((bf16[1,40,2048]{2,1,0:T(8,128)(2,1)S(1)}, bf16[1,40,2048]{2,1,0:T(8,128)(2,1)S(1)}, u32[]{:S(2)}, u32[]{:S(2)}) %collective-permute-start.26) | collective-permute-done | bytes 163872 | tf_op jit(solution)/shard_map/ppermute | solution.py:37
  459.9 3.0 gather_fusion.7
  462.9 6.1 %pad_maximum_fusion = bf16[8,160,2048]{2,1,0:T(8,128)(2,1)} fusion(bf16[8,40,2048]{2,1,0:T(8,128)(2,1)} %gather_fusion.7, bf16[8,40,2048]{2,1,0:T(8,128)(2,1)} %gather_fusion.5, bf16[8,40,2048]{2,1,0:T(8,128)(2,1)S(1)} %gather_fusion.3, bf16[8,40,2048]{2,1,0:T(8,128)(2,1)S(1)} %gather_fusion.1), kind=kLoop, calls=%fused_computation.18 | loop fusion | flops 20971520 | bytes 10485760 | tf_op jit(solution)/shard_map/concatenate | solution.py:116
  469.0 12.0 %gather_fusion.8 = bf16[1024,2048]{1,0:T(8,128)(2,1)} fusion(bf16[1280,2048]{1,0:T(8,128)(2,1)} %bitcast.322, s32[1024]{0:T(1024)S(1)} %broadcast_clamp_fusion), kind=kCustom, calls=%fused_computation.8 | custom fusion | bytes 8392704 | tf_op jit(solution)/shard_map/jit(_take)/gather | solution.py:117
  481.0 3.5 fusion.8
  (181 shorter events, 52.0 us)
Async XLA Ops:
  6.5 132.2 %all-gather.2.cloned.1.call-start = ((), (), s32[]{:S(2)}) async-start(), calls=%async_computation.4 | async-start | bytes 18382848 | tf_op jit(solution)/shard_map/all_gather | solution.py:86
  10.0 4.9 %copy-start = (bf16[128,2048]{1,0:T(8,128)(2,1)S(1)}, bf16[128,2048]{1,0:T(8,128)(2,1)}, u32[]{:S(2)}) copy-start(bf16[128,2048]{1,0:T(8,128)(2,1)} %param.8) | copy-start | bytes 1572868
  10.0 4.9 %copy-start.6 = (f32[2048]{0:T(1024)S(1)}, f32[2048]{0:T(1024)}, u32[]{:S(2)}) copy-start(f32[2048]{0:T(1024)} %param.9) | copy-start | bytes 24580
  16.1 208.2 %reduce-scatter.5.cloned.1.call-start = ((), (), s32[]{:S(2)}) async-start(), calls=%async_computation.5 | async-start | bytes 6553600 | tf_op jit(solution)/shard_map/reduce_scatter | solution.py:112
  174.1 121.6 %reduce-scatter.7.cloned.1.call-start = ((), (), s32[]{:S(2)}) async-start(), calls=%async_computation.6 | async-start | bytes 6553600 | tf_op jit(solution)/shard_map/reduce_scatter | solution.py:112
  224.3 144.6 %reduce-scatter.9.cloned.1.call-start = ((), (), s32[]{:S(2)}) async-start(), calls=%async_computation.7 | async-start | bytes 6553600 | tf_op jit(solution)/shard_map/reduce_scatter | solution.py:112
  253.0 5.9 %copy-start.3 = (bf16[4,80,2048]{2,1,0:T(8,128)(2,1)S(1)}, bf16[4,80,2048]{2,1,0:T(8,128)(2,1)}, u32[]{:S(2)}) copy-start(bf16[4,80,2048]{2,1,0:T(8,128)(2,1)} %reduce-scatter.5.cloned.1.call-done) | copy-start | bytes 3932164
  264.2 10.3 %collective-permute-start = (bf16[1,40,2048]{2,1,0:T(8,128)(2,1)S(1)}, bf16[1,40,2048]{2,1,0:T(8,128)(2,1)S(1)}, u32[]{:S(2)}, u32[]{:S(2)}) collective-permute-start(bf16[1,40,2048]{2,1,0:T(8,128)(2,1)S(1)} %bitcast.364), channel_id=1, source_target_pairs={{0,4},{4,0},{8,12},{12,8},{16,20},{20,16},{24,28},{28,24},{1,5},{5... | collective-permute-start | bytes 491528 | tf_op jit(solution)/shard_map/ppermute | solution.py:37
  265.1 15.1 %collective-permute-start.1 = (bf16[1,40,2048]{2,1,0:T(8,128)(2,1)S(1)}, bf16[1,40,2048]{2,1,0:T(8,128)(2,1)S(1)}, u32[]{:S(2)}, u32[]{:S(2)}) collective-permute-start(bf16[1,40,2048]{2,1,0:T(8,128)(2,1)S(1)} %bitcast.360), channel_id=1, source_target_pairs={{0,8},{4,12},{8,0},{12,4},{16,24},{20,28},{24,16},{28,20},{1,9},{5... | collective-permute-start | bytes 491528 | tf_op jit(solution)/shard_map/ppermute | solution.py:37
  267.5 16.0 %collective-permute-start.2 = (bf16[1,40,2048]{2,1,0:T(8,128)(2,1)S(1)}, bf16[1,40,2048]{2,1,0:T(8,128)(2,1)S(1)}, u32[]{:S(2)}, u32[]{:S(2)}) collective-permute-start(bf16[1,40,2048]{2,1,0:T(8,128)(2,1)S(1)} %bitcast.348), channel_id=1, source_target_pairs={{0,12},{4,8},{8,4},{12,0},{16,28},{20,24},{24,20},{28,16},{1,13},{... | collective-permute-start | bytes 491528 | tf_op jit(solution)/shard_map/ppermute | solution.py:37
  268.6 14.9 %collective-permute-start.3 = (bf16[1,40,2048]{2,1,0:T(8,128)(2,1)S(1)}, bf16[1,40,2048]{2,1,0:T(8,128)(2,1)S(1)}, u32[]{:S(2)}, u32[]{:S(2)}) collective-permute-start(bf16[1,40,2048]{2,1,0:T(8,128)(2,1)S(1)} %bitcast.344), channel_id=1, source_target_pairs={{0,16},{4,20},{8,24},{12,28},{16,0},{20,4},{24,8},{28,12},{1,17},{... | collective-permute-start | bytes 491528 | tf_op jit(solution)/shard_map/ppermute | solution.py:37
  269.5 14.1 %collective-permute-start.4 = (bf16[1,40,2048]{2,1,0:T(8,128)(2,1)S(1)}, bf16[1,40,2048]{2,1,0:T(8,128)(2,1)S(1)}, u32[]{:S(2)}, u32[]{:S(2)}) collective-permute-start(bf16[1,40,2048]{2,1,0:T(8,128)(2,1)S(1)} %bitcast.340), channel_id=1, source_target_pairs={{0,20},{4,16},{8,28},{12,24},{16,4},{20,0},{24,12},{28,8},{1,21},{... | collective-permute-start | bytes 491528 | tf_op jit(solution)/shard_map/ppermute | solution.py:37
  274.5 20.6 %collective-permute-start.5 = (bf16[1,40,2048]{2,1,0:T(8,128)(2,1)S(1)}, bf16[1,40,2048]{2,1,0:T(8,128)(2,1)S(1)}, u32[]{:S(2)}, u32[]{:S(2)}) collective-permute-start(bf16[1,40,2048]{2,1,0:T(8,128)(2,1)S(1)} %bitcast.356), channel_id=1, source_target_pairs={{0,24},{4,28},{8,16},{12,20},{16,8},{20,12},{24,0},{28,4},{1,25},{... | collective-permute-start | bytes 491528 | tf_op jit(solution)/shard_map/ppermute | solution.py:37
  280.2 14.9 %collective-permute-start.6 = (bf16[1,40,2048]{2,1,0:T(8,128)(2,1)S(1)}, bf16[1,40,2048]{2,1,0:T(8,128)(2,1)S(1)}, u32[]{:S(2)}, u32[]{:S(2)}) collective-permute-start(bf16[1,40,2048]{2,1,0:T(8,128)(2,1)S(1)} %bitcast.349), channel_id=1, source_target_pairs={{0,28},{4,24},{8,20},{12,16},{16,12},{20,8},{24,4},{28,0},{1,29},{... | collective-permute-start | bytes 491528 | tf_op jit(solution)/shard_map/ppermute | solution.py:37
  295.8 124.6 %reduce-scatter.11.cloned.1.call-start = ((), (), s32[]{:S(2)}) async-start(), calls=%async_computation.8 | async-start | bytes 6553600 | tf_op jit(solution)/shard_map/reduce_scatter | solution.py:112
  323.9 6.0 %copy-start.2 = (bf16[4,80,2048]{2,1,0:T(8,128)(2,1)S(1)}, bf16[4,80,2048]{2,1,0:T(8,128)(2,1)}, u32[]{:S(2)}) copy-start(bf16[4,80,2048]{2,1,0:T(8,128)(2,1)} %reduce-scatter.7.cloned.1.call-done) | copy-start | bytes 3932164
  335.2 9.0 %collective-permute-start.7 = (bf16[1,40,2048]{2,1,0:T(8,128)(2,1)S(1)}, bf16[1,40,2048]{2,1,0:T(8,128)(2,1)S(1)}, u32[]{:S(2)}, u32[]{:S(2)}) collective-permute-start(bf16[1,40,2048]{2,1,0:T(8,128)(2,1)S(1)} %bitcast.365), channel_id=1, source_target_pairs={{0,4},{4,0},{8,12},{12,8},{16,20},{20,16},{24,28},{28,24},{1,5},{5... | collective-permute-start | bytes 491528 | tf_op jit(solution)/shard_map/ppermute | solution.py:37
  337.8 15.1 %collective-permute-start.8 = (bf16[1,40,2048]{2,1,0:T(8,128)(2,1)S(1)}, bf16[1,40,2048]{2,1,0:T(8,128)(2,1)S(1)}, u32[]{:S(2)}, u32[]{:S(2)}) collective-permute-start(bf16[1,40,2048]{2,1,0:T(8,128)(2,1)S(1)} %bitcast.361), channel_id=1, source_target_pairs={{0,8},{4,12},{8,0},{12,4},{16,24},{20,28},{24,16},{28,20},{1,9},{5... | collective-permute-start | bytes 491528 | tf_op jit(solution)/shard_map/ppermute | solution.py:37
  338.7 16.4 %collective-permute-start.9 = (bf16[1,40,2048]{2,1,0:T(8,128)(2,1)S(1)}, bf16[1,40,2048]{2,1,0:T(8,128)(2,1)S(1)}, u32[]{:S(2)}, u32[]{:S(2)}) collective-permute-start(bf16[1,40,2048]{2,1,0:T(8,128)(2,1)S(1)} %bitcast.350), channel_id=1, source_target_pairs={{0,12},{4,8},{8,4},{12,0},{16,28},{20,24},{24,20},{28,16},{1,13},{... | collective-permute-start | bytes 491528 | tf_op jit(solution)/shard_map/ppermute | solution.py:37
  340.3 14.9 %collective-permute-start.10 = (bf16[1,40,2048]{2,1,0:T(8,128)(2,1)S(1)}, bf16[1,40,2048]{2,1,0:T(8,128)(2,1)S(1)}, u32[]{:S(2)}, u32[]{:S(2)}) collective-permute-start(bf16[1,40,2048]{2,1,0:T(8,128)(2,1)S(1)} %bitcast.345), channel_id=1, source_target_pairs={{0,16},{4,20},{8,24},{12,28},{16,0},{20,4},{24,8},{28,12},{1,17},{... | collective-permute-start | bytes 491528 | tf_op jit(solution)/shard_map/ppermute | solution.py:37
  340.7 14.5 %collective-permute-start.11 = (bf16[1,40,2048]{2,1,0:T(8,128)(2,1)S(1)}, bf16[1,40,2048]{2,1,0:T(8,128)(2,1)S(1)}, u32[]{:S(2)}, u32[]{:S(2)}) collective-permute-start(bf16[1,40,2048]{2,1,0:T(8,128)(2,1)S(1)} %bitcast.341), channel_id=1, source_target_pairs={{0,20},{4,16},{8,28},{12,24},{16,4},{20,0},{24,12},{28,8},{1,21},{... | collective-permute-start | bytes 491528 | tf_op jit(solution)/shard_map/ppermute | solution.py:37
  344.1 21.7 %collective-permute-start.12 = (bf16[1,40,2048]{2,1,0:T(8,128)(2,1)S(1)}, bf16[1,40,2048]{2,1,0:T(8,128)(2,1)S(1)}, u32[]{:S(2)}, u32[]{:S(2)}) collective-permute-start(bf16[1,40,2048]{2,1,0:T(8,128)(2,1)S(1)} %bitcast.357), channel_id=1, source_target_pairs={{0,24},{4,28},{8,16},{12,20},{16,8},{20,12},{24,0},{28,4},{1,25},{... | collective-permute-start | bytes 491528 | tf_op jit(solution)/shard_map/ppermute | solution.py:37
  353.0 12.8 %collective-permute-start.13 = (bf16[1,40,2048]{2,1,0:T(8,128)(2,1)S(1)}, bf16[1,40,2048]{2,1,0:T(8,128)(2,1)S(1)}, u32[]{:S(2)}, u32[]{:S(2)}) collective-permute-start(bf16[1,40,2048]{2,1,0:T(8,128)(2,1)S(1)} %bitcast.351), channel_id=1, source_target_pairs={{0,28},{4,24},{8,20},{12,16},{16,12},{20,8},{24,4},{28,0},{1,29},{... | collective-permute-start | bytes 491528 | tf_op jit(solution)/shard_map/ppermute | solution.py:37
  365.8 1.1 copy-start.1
  368.9 0.7 copy-start.5
  368.9 0.9 copy-start.4
  376.7 8.3 %collective-permute-start.14 = (bf16[1,40,2048]{2,1,0:T(8,128)(2,1)S(1)}, bf16[1,40,2048]{2,1,0:T(8,128)(2,1)S(1)}, u32[]{:S(2)}, u32[]{:S(2)}) collective-permute-start(bf16[1,40,2048]{2,1,0:T(8,128)(2,1)S(1)} %bitcast.366), channel_id=1, source_target_pairs={{0,4},{4,0},{8,12},{12,8},{16,20},{20,16},{24,28},{28,24},{1,5},{5... | collective-permute-start | bytes 491528 | tf_op jit(solution)/shard_map/ppermute | solution.py:37
  379.1 15.1 %collective-permute-start.15 = (bf16[1,40,2048]{2,1,0:T(8,128)(2,1)S(1)}, bf16[1,40,2048]{2,1,0:T(8,128)(2,1)S(1)}, u32[]{:S(2)}, u32[]{:S(2)}) collective-permute-start(bf16[1,40,2048]{2,1,0:T(8,128)(2,1)S(1)} %bitcast.362), channel_id=1, source_target_pairs={{0,8},{4,12},{8,0},{12,4},{16,24},{20,28},{24,16},{28,20},{1,9},{5... | collective-permute-start | bytes 491528 | tf_op jit(solution)/shard_map/ppermute | solution.py:37
  380.0 18.2 %collective-permute-start.16 = (bf16[1,40,2048]{2,1,0:T(8,128)(2,1)S(1)}, bf16[1,40,2048]{2,1,0:T(8,128)(2,1)S(1)}, u32[]{:S(2)}, u32[]{:S(2)}) collective-permute-start(bf16[1,40,2048]{2,1,0:T(8,128)(2,1)S(1)} %bitcast.352), channel_id=1, source_target_pairs={{0,12},{4,8},{8,4},{12,0},{16,28},{20,24},{24,20},{28,16},{1,13},{... | collective-permute-start | bytes 491528 | tf_op jit(solution)/shard_map/ppermute | solution.py:37
  381.5 17.4 %collective-permute-start.17 = (bf16[1,40,2048]{2,1,0:T(8,128)(2,1)S(1)}, bf16[1,40,2048]{2,1,0:T(8,128)(2,1)S(1)}, u32[]{:S(2)}, u32[]{:S(2)}) collective-permute-start(bf16[1,40,2048]{2,1,0:T(8,128)(2,1)S(1)} %bitcast.346), channel_id=1, source_target_pairs={{0,16},{4,20},{8,24},{12,28},{16,0},{20,4},{24,8},{28,12},{1,17},{... | collective-permute-start | bytes 491528 | tf_op jit(solution)/shard_map/ppermute | solution.py:37
  383.0 16.6 %collective-permute-start.18 = (bf16[1,40,2048]{2,1,0:T(8,128)(2,1)S(1)}, bf16[1,40,2048]{2,1,0:T(8,128)(2,1)S(1)}, u32[]{:S(2)}, u32[]{:S(2)}) collective-permute-start(bf16[1,40,2048]{2,1,0:T(8,128)(2,1)S(1)} %bitcast.342), channel_id=1, source_target_pairs={{0,20},{4,16},{8,28},{12,24},{16,4},{20,0},{24,12},{28,8},{1,21},{... | collective-permute-start | bytes 491528 | tf_op jit(solution)/shard_map/ppermute | solution.py:37
  385.0 23.0 %collective-permute-start.19 = (bf16[1,40,2048]{2,1,0:T(8,128)(2,1)S(1)}, bf16[1,40,2048]{2,1,0:T(8,128)(2,1)S(1)}, u32[]{:S(2)}, u32[]{:S(2)}) collective-permute-start(bf16[1,40,2048]{2,1,0:T(8,128)(2,1)S(1)} %bitcast.358), channel_id=1, source_target_pairs={{0,24},{4,28},{8,16},{12,20},{16,8},{20,12},{24,0},{28,4},{1,25},{... | collective-permute-start | bytes 491528 | tf_op jit(solution)/shard_map/ppermute | solution.py:37
  394.1 14.6 %collective-permute-start.20 = (bf16[1,40,2048]{2,1,0:T(8,128)(2,1)S(1)}, bf16[1,40,2048]{2,1,0:T(8,128)(2,1)S(1)}, u32[]{:S(2)}, u32[]{:S(2)}) collective-permute-start(bf16[1,40,2048]{2,1,0:T(8,128)(2,1)S(1)} %bitcast.353), channel_id=1, source_target_pairs={{0,28},{4,24},{8,20},{12,16},{16,12},{20,8},{24,4},{28,0},{1,29},{... | collective-permute-start | bytes 491528 | tf_op jit(solution)/shard_map/ppermute | solution.py:37
  427.0 9.6 %collective-permute-start.21 = (bf16[1,40,2048]{2,1,0:T(8,128)(2,1)S(1)}, bf16[1,40,2048]{2,1,0:T(8,128)(2,1)S(1)}, u32[]{:S(2)}, u32[]{:S(2)}) collective-permute-start(bf16[1,40,2048]{2,1,0:T(8,128)(2,1)S(1)} %bitcast.367), channel_id=1, source_target_pairs={{0,4},{4,0},{8,12},{12,8},{16,20},{20,16},{24,28},{28,24},{1,5},{5... | collective-permute-start | bytes 491528 | tf_op jit(solution)/shard_map/ppermute | solution.py:37
  428.5 15.1 %collective-permute-start.22 = (bf16[1,40,2048]{2,1,0:T(8,128)(2,1)S(1)}, bf16[1,40,2048]{2,1,0:T(8,128)(2,1)S(1)}, u32[]{:S(2)}, u32[]{:S(2)}) collective-permute-start(bf16[1,40,2048]{2,1,0:T(8,128)(2,1)S(1)} %bitcast.363), channel_id=1, source_target_pairs={{0,8},{4,12},{8,0},{12,4},{16,24},{20,28},{24,16},{28,20},{1,9},{5... | collective-permute-start | bytes 491528 | tf_op jit(solution)/shard_map/ppermute | solution.py:37
  430.9 16.7 %collective-permute-start.23 = (bf16[1,40,2048]{2,1,0:T(8,128)(2,1)S(1)}, bf16[1,40,2048]{2,1,0:T(8,128)(2,1)S(1)}, u32[]{:S(2)}, u32[]{:S(2)}) collective-permute-start(bf16[1,40,2048]{2,1,0:T(8,128)(2,1)S(1)} %bitcast.354), channel_id=1, source_target_pairs={{0,12},{4,8},{8,4},{12,0},{16,28},{20,24},{24,20},{28,16},{1,13},{... | collective-permute-start | bytes 491528 | tf_op jit(solution)/shard_map/ppermute | solution.py:37
  431.4 16.9 %collective-permute-start.24 = (bf16[1,40,2048]{2,1,0:T(8,128)(2,1)S(1)}, bf16[1,40,2048]{2,1,0:T(8,128)(2,1)S(1)}, u32[]{:S(2)}, u32[]{:S(2)}) collective-permute-start(bf16[1,40,2048]{2,1,0:T(8,128)(2,1)S(1)} %bitcast.347), channel_id=1, source_target_pairs={{0,16},{4,20},{8,24},{12,28},{16,0},{20,4},{24,8},{28,12},{1,17},{... | collective-permute-start | bytes 491528 | tf_op jit(solution)/shard_map/ppermute | solution.py:37
  432.9 16.1 %collective-permute-start.25 = (bf16[1,40,2048]{2,1,0:T(8,128)(2,1)S(1)}, bf16[1,40,2048]{2,1,0:T(8,128)(2,1)S(1)}, u32[]{:S(2)}, u32[]{:S(2)}) collective-permute-start(bf16[1,40,2048]{2,1,0:T(8,128)(2,1)S(1)} %bitcast.343), channel_id=1, source_target_pairs={{0,20},{4,16},{8,28},{12,24},{16,4},{20,0},{24,12},{28,8},{1,21},{... | collective-permute-start | bytes 491528 | tf_op jit(solution)/shard_map/ppermute | solution.py:37
  436.6 21.9 %collective-permute-start.26 = (bf16[1,40,2048]{2,1,0:T(8,128)(2,1)S(1)}, bf16[1,40,2048]{2,1,0:T(8,128)(2,1)S(1)}, u32[]{:S(2)}, u32[]{:S(2)}) collective-permute-start(bf16[1,40,2048]{2,1,0:T(8,128)(2,1)S(1)} %bitcast.359), channel_id=1, source_target_pairs={{0,24},{4,28},{8,16},{12,20},{16,8},{20,12},{24,0},{28,4},{1,25},{... | collective-permute-start | bytes 491528 | tf_op jit(solution)/shard_map/ppermute | solution.py:37
  443.6 15.6 %collective-permute-start.27 = (bf16[1,40,2048]{2,1,0:T(8,128)(2,1)S(1)}, bf16[1,40,2048]{2,1,0:T(8,128)(2,1)S(1)}, u32[]{:S(2)}, u32[]{:S(2)}) collective-permute-start(bf16[1,40,2048]{2,1,0:T(8,128)(2,1)S(1)} %bitcast.355), channel_id=1, source_target_pairs={{0,28},{4,24},{8,20},{12,16},{16,12},{20,8},{24,4},{28,0},{1,29},{... | collective-permute-start | bytes 491528 | tf_op jit(solution)/shard_map/ppermute | solution.py:37
Sparse Core Ops, SparseCore 0:
  16.2 122.5 all-gather.1
  174.3 49.5 reduce-scatter.4
  226.6 51.4 reduce-scatter.6
  295.9 50.3 reduce-scatter.8
  369.1 51.2 reduce-scatter.10
